TPU v7x, 128 devices: a whole 4x4x4 slice. The times are simulated.
128 devices in a mesh: row: 64 (over y, x, z_lo, core), col: 2 (over z_hi).
Axes of the slice: x: 4, y: 4, z: 4 (z_hi: 2, z_lo: 2; z = z_hi * 2 + z_lo), core: 2. Of those that a mesh axis runs over, the one named last changes fastest.
Arguments:
- dist_first: bfloat16 [32768, 32768], P('row', 'col'), may hold values from -0.34 to 0.34
- coupling: bfloat16 [32768, 256], P('row', 'col'), may hold values from 0.099609375 to 1
- dist_second: bfloat16 [256, 512], P(None, 'col'), may hold values from -12 to 12
- row_potential: float32 [32768], P('row'), may hold values from -150 to 120
- column_cost: float32 [512], P('col'), may hold values from -300 to 20
- column_mass: float32 [512], P('col'), may hold values from 0.5 to 2
Outputs:
- transport: bfloat16 [32768, 512], P('row', 'col')
- potential: float32 [512], P('col')
All inputs are finite; a program needn't handle non-finite values.
Results may differ from a plain program's by a relative error of at most 0.0051.
Values may be sent and summed in bfloat16 or wider, within the bound.
No kernel may reach another device: no remote copies, remote signals or barrier semaphores. Data moves between devices by JAX's collectives and lax.ppermute only.
A program may use at most 128 MiB of HBM per device.

v0:
```python
import jax
import jax.numpy as jnp
from jax import lax
from jax.sharding import PartitionSpec as P

N = 32768


def joined_along(blocks, dim):
    shape = list(blocks.shape[1:])
    shape[dim] *= blocks.shape[0]
    return jnp.moveaxis(blocks, 0, dim).reshape(shape)


def copy_for_each(array, axis):
    copies = jnp.broadcast_to(array, (lax.axis_size(axis), *array.shape))
    return lax.all_to_all(copies, axis, split_axis=0, concat_axis=0, tiled=True)


def gather_directly(array, axis, dim):
    return joined_along(copy_for_each(array, axis), dim)


def split_up(array, dim, length):
    shape = array.shape
    blocks = array.reshape(*shape[:dim], length, shape[dim] // length, *shape[dim + 1 :])
    return jnp.moveaxis(blocks, dim, 0)


def summed_on_arrival(array, axis, dim):
    length = lax.axis_size(axis)
    blocks = lax.all_to_all(split_up(array, dim, length), axis, 0, 0, tiled=True)
    return jnp.sum(blocks, axis=0)


def all_in_one(array, axis):
    leaves = jax.tree.leaves(array)
    sequence = sorted(range(len(leaves)), key=lambda k: -leaves[k].size)
    width = (1, *leaves[sequence[0]].shape)[-1]
    lines = [
        jnp.pad(leaves[k].reshape(-1), (0, -leaves[k].size % width)).reshape(-1, width)
        for k in sequence
    ]
    both, at, found = (copy_for_each(jnp.concatenate(lines), axis), 0, {})
    for k, line in zip(sequence, lines):
        section = both[:, at : at + len(line)].reshape(len(both), -1)
        found[k] = section[:, : leaves[k].size].reshape(-1, *leaves[k].shape)
        at += len(line)
    numbers = iter(range(len(leaves)))
    return jax.tree.map(lambda _: found[next(numbers)], array)


def combined_pairwise(pieces, combine):
    while len(jax.tree.leaves(pieces)[0]) > 1:
        pieces = jax.vmap(combine)(
            *(jax.tree.map(lambda part: part[side::2], pieces) for side in (0, 1))
        )
    return jax.tree.map(lambda part: part[0], pieces)


def merged(array, axis, combine):
    pieces = all_in_one(array, axis)
    return combined_pairwise(pieces, combine)


def merge_columns(earlier, later):
    highest = jnp.maximum(earlier[0], later[0])
    summed = earlier[1] * jnp.exp(earlier[0] - highest) + later[1] * jnp.exp(later[0] - highest)
    return (highest, summed)


def body(dist_first, coupling, dist_second, row_potential, column_cost, column_mass):
    groups = lax.axis_size("col")
    stacked = lax.all_gather(coupling, "row", axis=0, tiled=True)
    total_rows = stacked.shape[0]
    stacked = stacked.reshape(groups, 1, total_rows // groups, stacked.shape[1])
    traded = lax.all_to_all(stacked, "col", split_axis=0, concat_axis=1, tiled=True)
    second_full = gather_directly(dist_second, "col", 1)
    second_blocks = second_full.reshape(
        groups, second_full.shape[0] // groups, second_full.shape[1]
    )
    product = jnp.einsum(
        "jnk,jkq->nq", traded[0], second_blocks, preferred_element_type=jnp.float32
    ).astype(jnp.bfloat16)
    partial_value = jnp.dot(dist_first, product, preferred_element_type=jnp.float32)
    gradient = summed_on_arrival(partial_value, "col", 1)
    scores = row_potential[:, None] + 2.0 * gradient - column_cost[None, :]
    local_high = jnp.max(scores, axis=0)
    local_sum = jnp.sum(jnp.exp(scores - local_high[None, :]), axis=0)
    highest, column_sum = merged((local_high, local_sum), "row", merge_columns)
    weights = jnp.exp(scores - highest[None, :])
    potential = jnp.log(column_mass) - highest - jnp.log(column_sum)
    transport = (weights * (N * column_mass / column_sum)[None, :]).astype(jnp.bfloat16)
    return (transport, potential)


def solution(mesh):
    in_specs = (P("row", "col"), P("row", "col"), P(None, "col"), P("row"), P("col"), P("col"))
    out_specs = (P("row", "col"), P("col"))
    return jax.shard_map(body, mesh=mesh, in_specs=in_specs, out_specs=out_specs, check_vma=False)
```

profile of v0, /device:TPU:1, one launch (start us, length us, event | category | flops | bytes accessed | tf_op | source)
XLA Modules:
  0.0 284.0 jit_solution(13788722296052831946)
XLA Ops:
  7.2 0.0 all-gather.2.cloned.1.call-start
  7.2 0.7 all-gather.2.cloned.1.call-update
  7.9 0.9 broadcast_in_dim.4
  8.8 11.0 %all_to_all.24 = bf16[2,256,256]{2,1,0:T(8,128)(2,1)S(1)} all-to-all(bf16[2,256,256]{2,1,0:T(8,128)(2,1)S(1)} %broadcast_in_dim.4), channel_id=1, replica_groups=mesh['row'=64,'col'=2] {'col'}, dimensions={0} | all-to-all | bytes 524288 | tf_op jit(solution)/shard_map/all_to_all | solution.py:17
  19.8 104.5 %all-gather.2.cloned.1.call-done = bf16[32768,128]{1,0:T(8,128)(2,1)} async-done(((bf16[512,128]{1,0:T(8,128)(2,1)}), bf16[32768,128]{1,0:T(8,128)(2,1)}) %all-gather.2.cloned.1.call-update) | async-done | bytes 8388624 | tf_op jit(solution)/shard_map/all_gather | solution.py:74
  124.4 6.9 %all-to-all-start = ((bf16[2,1,16384,128]{3,2,1,0:T(8,128)(2,1)}), bf16[2,1,16384,128]{3,2,1,0:T(8,128)(2,1)}, u32[]{:S(2)}, u32[]{:S(2)}) async-start(bf16[2,1,16384,128]{3,2,1,0:T(8,128)(2,1)} %bitcast.26), calls=%async_computation | async-start | bytes 16777216 | tf_op jit(solution)/shard_map/all_to_all | solution.py:77
  131.3 0.3 copy.10
  131.6 0.2 reshape_reshape.3
  131.8 0.0 copy-start
  131.8 0.0 copy-start.1
  131.8 0.0 copy-start.2
  131.8 93.2 %all-to-all-done = bf16[2,1,16384,128]{3,2,1,0:T(8,128)(2,1)} async-done(((bf16[2,1,16384,128]{3,2,1,0:T(8,128)(2,1)}), bf16[2,1,16384,128]{3,2,1,0:T(8,128)(2,1)}, u32[]{:S(2)}, u32[]{:S(2)}) %all-to-all-start) | async-done | bytes 8388640 | tf_op jit(solution)/shard_map/all_to_all | solution.py:77
  225.0 16.6 %fusion.2 = f32[512,512]{1,0:T(8,128)S(1)} fusion(bf16[512,16384]{1,0:T(8,128)(2,1)} %param.6, bf16[2,128,512]{2,1,0:T(8,128)(2,1)S(1)} %reshape_reshape.3, bf16[2,1,16384,128]{3,2,1,0:T(8,128)(2,1)} %all-to-all-done), kind=kOutput, calls=%fused_computation.2 | convolution fusion | flops 12893290496 | bytes 26476544 | tf_op jit(solution)/shard_map/dot_general | solution.py:85
  241.6 16.5 %all_to_all.25 = f32[2,512,256]{1,2,0:T(8,128)S(1)} all-to-all(f32[2,512,256]{1,2,0:T(8,128)S(1)} %bitcast.27), channel_id=1, replica_groups=mesh['row'=64,'col'=2] {'col'}, dimensions={0} | all-to-all | bytes 2097152 | tf_op jit(solution)/shard_map/all_to_all | solution.py:32
  258.1 0.1 reduce_sum.18
  258.2 0.0 copy-done
  258.2 0.0 copy-done.1
  258.2 0.2 fusion.4
  258.4 0.2 exponential_reduce_fusion
  258.7 16.2 %all_to_all.26 = f32[64,2,256]{2,1,0:T(2,128)S(1)} all-to-all(f32[64,2,256]{2,1,0:T(2,128)S(1)} %broadcast_in_dim.5), channel_id=1, replica_groups=mesh['row'=64,'col'=2] {'row'}, dimensions={0} | all-to-all | bytes 262144 | tf_op jit(solution)/shard_map/all_to_all | solution.py:17
  274.9 0.1 fusion.6
  275.6 0.0 copy-done.2
  275.6 0.6 log_subtract_fusion
  276.2 0.2 multiply_convert_fusion
  276.4 0.8 copy.12
  (29 shorter events, 0.5 us)
Async XLA Ops:
  7.2 117.2 %all-gather.2.cloned.1.call-start = ((), (), s32[]{:S(2)}) async-start(), calls=%async_computation.4 | async-start | bytes 8519680 | tf_op jit(solution)/shard_map/all_gather | solution.py:74
  124.4 100.6 %all-to-all-start = ((bf16[2,1,16384,128]{3,2,1,0:T(8,128)(2,1)}), bf16[2,1,16384,128]{3,2,1,0:T(8,128)(2,1)}, u32[]{:S(2)}, u32[]{:S(2)}) async-start(bf16[2,1,16384,128]{3,2,1,0:T(8,128)(2,1)} %bitcast.26), calls=%async_computation | async-start | bytes 16777216 | tf_op jit(solution)/shard_map/all_to_all | solution.py:77
  131.8 126.4 %copy-start = (f32[512]{0:T(512)S(1)}, f32[512]{0:T(512)}, u32[]{:S(2)}) copy-start(f32[512]{0:T(512)} %param.9) | copy-start | bytes 6148
  131.8 126.4 %copy-start.1 = (f32[256]{0:T(256)S(1)}, f32[256]{0:T(256)}, u32[]{:S(2)}) copy-start(f32[256]{0:T(256)} %param.10) | copy-start | bytes 3076
  131.8 143.8 %copy-start.2 = (f32[256]{0:T(256)S(1)}, f32[256]{0:T(256)}, u32[]{:S(2)}) copy-start(f32[256]{0:T(256)} %param.11) | copy-start | bytes 3076
Sparse Core Ops, SparseCore 0:
  9.7 114.6 all-gather.1
where the time goes:
time: 284 us
  waiting for transfers between devices  198 us (70%)
  blocking collectives  43.7 us (15%)
  matrix products  16.6 us (6%)
  between operations  14.2 us (5%)
  starting transfers between devices  6.97 us (2%)
    all_gather x1, waiting for transfers between devices, body(): stacked = lax.all_gather(coupling, 'row', axis=0, tiled=True)  105 us
    all_to_all x1, waiting for transfers between devices, body(): lax.all_to_all(stacked, 'col', split_axis=0, concat_axis=1, tiled=True)  93.2 us
    all_to_all x2, blocking collectives, copy_for_each(): return lax.all_to_all(copies, axis, split_axis=0, concat_axis=0, tiled=True)  27.2 us
    dot_general x1, matrix products, body(): jnp.dot(dist_first, product, preferred_element_type=jnp.float32)  16.6 us
    all_to_all x1, blocking collectives, summed_on_arrival(): lax.all_to_all(split_up(array, dim, length), axis, 0, 0, tiled=True)  16.5 us
    all_to_all x1, starting transfers between devices, body(): lax.all_to_all(stacked, 'col', split_axis=0, concat_axis=1, tiled=True)  6.93 us
  transfers between devices with their start and end apart: 2, of which 2 were waited for; matrix products, arithmetic and copies ran while one was open for 0% of the time, Pallas kernels for 0%

commit v1 on v0

--- a/solution.py
+++ b/solution.py
@@ -71,7 +71,10 @@
 
 def body(dist_first, coupling, dist_second, row_potential, column_cost, column_mass):
     groups = lax.axis_size("col")
-    stacked = lax.all_gather(coupling, "row", axis=0, tiled=True)
+    peers = lax.axis_size("row")
+    parts = jnp.stack([coupling for _ in range(peers)])
+    parts = lax.all_to_all(parts, "row", split_axis=0, concat_axis=0)
+    stacked = jnp.concatenate(parts, axis=0)
     total_rows = stacked.shape[0]
     stacked = stacked.reshape(groups, 1, total_rows // groups, stacked.shape[1])
     traded = lax.all_to_all(stacked, "col", split_axis=0, concat_axis=1, tiled=True)

time: 284 us -> 274 us (0.965)
  blocking collectives: 43.7 us -> 149 us
  waiting for transfers between devices: 198 us -> 93.3 us
  between operations: 14.2 us -> 0.81 us
  local copies, waits for them, and re-layouts: 2.76 us -> 5.67 us
    all_to_all x0 -> x1, blocking collectives: none -> 106 us  [body(): parts = lax.all_to_all(parts, 'row', split_axis=0, concat_axis=0)]
    all_gather x1 -> x0, waiting for transfers between devices: 105 us -> none  [body(): stacked = lax.all_gather(coupling, 'row', axis=0, tiled=True)]
    another operation x0 -> x1, local copies, waits for them, and re-layouts: none -> 2.91 us  [body(): parts = jnp.stack([coupling for _ in range(peers)])]
  transfers between devices with their start and end apart: 2 -> 1, of which waited for: 2 -> 1; matrix products, arithmetic and copies ran while one was open for 0% -> 0% of each run, Pallas kernels for 0% -> 0%
where the time goes in v1:
time: 274 us
  blocking collectives  149 us (54%)
  waiting for transfers between devices  93.3 us (34%)
  matrix products  16.6 us (6%)
  starting transfers between devices  6.93 us (3%)
  local copies, waits for them, and re-layouts  5.67 us (2%)
    all_to_all x1, blocking collectives, body(): parts = lax.all_to_all(parts, 'row', split_axis=0, concat_axis=0)  106 us
    all_to_all x1, waiting for transfers between devices, body(): lax.all_to_all(stacked, 'col', split_axis=0, concat_axis=1, tiled=True)  93.3 us
    all_to_all x2, blocking collectives, copy_for_each(): return lax.all_to_all(copies, axis, split_axis=0, concat_axis=0, tiled=True)  25.9 us
    all_to_all x1, blocking collectives, summed_on_arrival(): lax.all_to_all(split_up(array, dim, length), axis, 0, 0, tiled=True)  16.6 us
    dot_general x1, matrix products, body(): jnp.dot(dist_first, product, preferred_element_type=jnp.float32)  16.6 us
    all_to_all x1, starting transfers between devices, body(): lax.all_to_all(stacked, 'col', split_axis=0, concat_axis=1, tiled=True)  6.93 us
  transfers between devices with their start and end apart: 1, of which 1 were waited for; matrix products, arithmetic and copies ran while one was open for 0% of the time, Pallas kernels for 0%

profile of v1, /device:TPU:1, one launch (start us, length us, event | category | flops | bytes accessed | tf_op | source)
XLA Modules:
  0.0 273.5 jit_solution(5199391143547492866)
XLA Ops:
  0.6 0.9 broadcast_in_dim.4
  1.6 11.0 %all_to_all.29 = bf16[2,256,256]{2,1,0:T(8,128)(2,1)S(1)} all-to-all(bf16[2,256,256]{2,1,0:T(8,128)(2,1)S(1)} %broadcast_in_dim.4), channel_id=1, replica_groups=mesh['row'=64,'col'=2] {'col'}, dimensions={0} | all-to-all | bytes 524288 | tf_op jit(solution)/shard_map/all_to_all | solution.py:17
  12.6 2.9 %stack.2 = bf16[64,512,128]{2,1,0:T(8,128)(2,1)S(1)} broadcast(bf16[512,128]{1,0:T(8,128)(2,1)} %param.7), dimensions={1,2} | broadcast | bytes 8519680 | tf_op jit(solution)/shard_map/stack | solution.py:75
  15.5 106.4 %all_to_all.30 = bf16[64,512,128]{2,1,0:T(8,128)(2,1)} all-to-all(bf16[64,512,128]{2,1,0:T(8,128)(2,1)S(1)} %stack.2), channel_id=1, replica_groups=mesh['row'=64,'col'=2] {'row'}, dimensions={0} | all-to-all | bytes 16777216 | tf_op jit(solution)/shard_map/all_to_all | solution.py:76
  121.9 6.9 %all-to-all-start.1 = ((bf16[2,1,16384,128]{3,2,1,0:T(8,128)(2,1)}), bf16[2,1,16384,128]{3,2,1,0:T(8,128)(2,1)}, u32[]{:S(2)}, u32[]{:S(2)}) async-start(bf16[2,1,16384,128]{3,2,1,0:T(8,128)(2,1)} %bitcast.26), calls=%async_computation.1 | async-start | bytes 16777216 | tf_op jit(solution)/shard_map/all_to_all | solution.py:80
  128.8 0.3 copy.10
  129.1 0.2 reshape_reshape.7
  129.3 0.0 copy-start
  129.3 0.0 copy-start.1
  129.3 0.0 copy-start.2
  129.3 93.3 %all-to-all-done.1 = bf16[2,1,16384,128]{3,2,1,0:T(8,128)(2,1)} async-done(((bf16[2,1,16384,128]{3,2,1,0:T(8,128)(2,1)}), bf16[2,1,16384,128]{3,2,1,0:T(8,128)(2,1)}, u32[]{:S(2)}, u32[]{:S(2)}) %all-to-all-start.1) | async-done | bytes 8388640 | tf_op jit(solution)/shard_map/all_to_all | solution.py:80
  222.6 16.6 %fusion.2 = f32[512,512]{1,0:T(8,128)S(1)} fusion(bf16[512,16384]{1,0:T(8,128)(2,1)} %param.6, bf16[2,128,512]{2,1,0:T(8,128)(2,1)S(1)} %reshape_reshape.7, bf16[2,1,16384,128]{3,2,1,0:T(8,128)(2,1)} %all-to-all-done.1), kind=kOutput, calls=%fused_computation.2 | convolution fusion | flops 12893290496 | bytes 26476544 | tf_op jit(solution)/shard_map/dot_general | solution.py:88
  239.2 16.6 %all_to_all.31 = f32[2,512,256]{1,2,0:T(8,128)S(1)} all-to-all(f32[2,512,256]{1,2,0:T(8,128)S(1)} %bitcast.27), channel_id=1, replica_groups=mesh['row'=64,'col'=2] {'col'}, dimensions={0} | all-to-all | bytes 2097152 | tf_op jit(solution)/shard_map/all_to_all | solution.py:32
  255.8 0.1 reduce_sum.18
  255.9 0.0 copy-done
  255.9 0.0 copy-done.1
  255.9 0.2 fusion.4
  256.1 0.2 exponential_reduce_fusion
  256.4 14.8 %all_to_all.32 = f32[64,2,256]{2,1,0:T(2,128)S(1)} all-to-all(f32[64,2,256]{2,1,0:T(2,128)S(1)} %broadcast_in_dim.5), channel_id=1, replica_groups=mesh['row'=64,'col'=2] {'row'}, dimensions={0} | all-to-all | bytes 262144 | tf_op jit(solution)/shard_map/all_to_all | solution.py:17
  271.2 0.1 fusion.6
  271.9 0.0 copy-done.2
  271.9 0.6 log_subtract_fusion
  272.5 0.2 multiply_convert_fusion
  272.7 0.8 copy.12
  (29 shorter events, 0.5 us)
Async XLA Ops:
  121.9 100.7 %all-to-all-start.1 = ((bf16[2,1,16384,128]{3,2,1,0:T(8,128)(2,1)}), bf16[2,1,16384,128]{3,2,1,0:T(8,128)(2,1)}, u32[]{:S(2)}, u32[]{:S(2)}) async-start(bf16[2,1,16384,128]{3,2,1,0:T(8,128)(2,1)} %bitcast.26), calls=%async_computation.1 | async-start | bytes 16777216 | tf_op jit(solution)/shard_map/all_to_all | solution.py:80
  129.3 126.6 %copy-start = (f32[512]{0:T(512)S(1)}, f32[512]{0:T(512)}, u32[]{:S(2)}) copy-start(f32[512]{0:T(512)} %param.9) | copy-start | bytes 6148
  129.3 126.6 %copy-start.1 = (f32[256]{0:T(256)S(1)}, f32[256]{0:T(256)}, u32[]{:S(2)}) copy-start(f32[256]{0:T(256)} %param.10) | copy-start | bytes 3076
  129.3 142.6 %copy-start.2 = (f32[256]{0:T(256)S(1)}, f32[256]{0:T(256)}, u32[]{:S(2)}) copy-start(f32[256]{0:T(256)} %param.11) | copy-start | bytes 3076
